TPU v7x, 512 devices: a whole 4x4x16 slice. The times are simulated.
512 devices in a mesh: row: 16 (over z), col: 32 (over y, x, core).
Axes of the slice: x: 4, y: 4, z: 16, core: 2. Of those that a mesh axis runs over, the one named last changes fastest.
Arguments:
- node_feats: bfloat16 [262144, 512], P(('row', 'col')), may hold values from -8 to 8
- source_feats: bfloat16 [4096, 512], P('col'), may hold values from -6 to 6
- nbr_blocks: int32 [2048, 8], P(('row', 'col')), may hold values from 0 to 31
- nbr_count: int32 [2048], P(('row', 'col')), may hold values from 1 to 8
- adj_tiles: bfloat16 [2048, 8, 128, 128], P(('row', 'col')), may hold values from -0.1875 to 0.1875
- pos_index: int32 [262144], P(('row', 'col')), may hold values from 0 to 511
- noise_block_rows: int32 [16], replicated, may hold values from 0 to 15
- w_self: bfloat16 [512, 512], replicated, may hold values from -0.25 to 0.25
- w_neigh: bfloat16 [512, 512], replicated, may hold values from -0.25 to 0.25
Outputs:
- grad_self: float32 [512, 512], replicated
- neighbour_weight_gradient: float32 [512, 512], replicated
- loss: float32 [], replicated
All inputs are finite; a program needn't handle non-finite values.
Results may differ from a plain program's by a relative error of at most 0.002.
Values may be sent and summed in bfloat16 or wider, within the bound.
No kernel may reach another device: no remote copies, remote signals or barrier semaphores. Data moves between devices by JAX's collectives and lax.ppermute only.
A program may use at most 64 MiB of HBM per device.

v0:
```python
import jax
import jax.numpy as jnp
from jax import lax
from jax.sharding import PartitionSpec as P

BLOCK = 128
NOISE = 128
softness_divisor = 0.2


def xor_pairs(size, mask):
    return [(i, i ^ mask) for i in range(size)]


REDUCE_STEPS = (
    ("col", 1),
    ("col", 2),
    ("col", 4),
    ("col", 8),
    ("col", 16),
    ("row", 1),
    ("row", 2),
    ("row", 4),
    ("row", 8),
)


def tree_allreduce(buf, extra):
    taken = []
    for axis, mask in REDUCE_STEPS:
        size = lax.axis_size(axis)
        if mask >= size:
            continue
        bit = lax.axis_index(axis) // mask % 2
        half = buf.shape[0] // 2
        keep = lax.dynamic_slice_in_dim(buf, bit * half, half, 0)
        send = lax.dynamic_slice_in_dim(buf, (1 - bit) * half, half, 0)
        got, got_extra = lax.ppermute((send, extra), axis, xor_pairs(size, mask))
        buf = keep + got
        extra = extra + got_extra
        taken.append((axis, mask, bit))
    for axis, mask, bit in reversed(taken):
        size = lax.axis_size(axis)
        got = lax.ppermute(buf, axis, xor_pairs(size, mask))
        rows = buf.shape[0]
        out = jnp.zeros((2 * rows,) + buf.shape[1:], buf.dtype)
        out = lax.dynamic_update_slice_in_dim(out, buf, bit * rows, 0)
        out = lax.dynamic_update_slice_in_dim(out, got, (1 - bit) * rows, 0)
        buf = out
    return (buf, extra)


def embed(pre):
    return pre * lax.rsqrt(jnp.sum(pre * pre, axis=-1, keepdims=True) + 1e-06)


def body(
    node_feats,
    source_feats,
    nbr_blocks,
    nbr_count,
    adj_tiles,
    pos_index,
    noise_block_rows,
    w_self,
    w_neigh,
):
    rows = node_feats.shape[0]
    width = node_feats.shape[1]
    slots = adj_tiles.shape[1]
    highest = lax.Precision.HIGHEST
    nodes = rows * lax.axis_size("row") * lax.axis_size("col")
    scale_factor = 1.0 / softness_divisor
    valid = jnp.arange(slots, dtype=jnp.int32)[None, :] < nbr_count[:, None]
    tiles = adj_tiles * valid[:, :, None, None].astype(jnp.bfloat16)
    piece = lax.all_gather(source_feats, "col", axis=0, tiled=True)
    count = piece.shape[0] // BLOCK
    blocks = piece.reshape(count, BLOCK, width)
    indicator_matrix = (
        nbr_blocks[:, :, None] == jnp.arange(count, dtype=jnp.int32)[None, None, :]
    ).astype(jnp.bfloat16)
    selected = jnp.einsum(
        "bkc,cjd->bkjd", indicator_matrix, blocks, preferred_element_type=jnp.float32
    ).astype(jnp.bfloat16)
    summed = jnp.einsum("bkij,bkjd->bid", tiles, selected, preferred_element_type=jnp.float32)
    agg = summed.reshape(rows, width).astype(jnp.bfloat16)
    pre = jnp.dot(node_feats, w_self, preferred_element_type=jnp.float32) + jnp.dot(
        agg, w_neigh, preferred_element_type=jnp.float32
    )
    emb32, pull = jax.vjp(embed, pre)
    zeta_bf = emb32.astype(jnp.bfloat16)
    candidates = lax.all_gather(zeta_bf[:NOISE], "row", axis=0, tiled=True)
    my_row = lax.axis_index("row")
    my_noise = noise_block_rows[my_row]
    noise_emb = lax.dynamic_slice_in_dim(candidates, my_noise * NOISE, NOISE, 0).astype(jnp.float32)
    zeta = zeta_bf.astype(jnp.float32)
    pairing = (pos_index[:, None] == jnp.arange(rows, dtype=jnp.int32)[None, :]).astype(jnp.float32)
    partner = jnp.dot(pairing, zeta, precision=highest)
    s_pos = jnp.sum(zeta * partner, axis=-1) * scale_factor
    s_neg = jnp.dot(zeta, noise_emb.T, precision=highest) * scale_factor
    loss_part = (jnp.sum(jax.nn.softplus(-s_pos)) + jnp.sum(jax.nn.softplus(s_neg)) / NOISE) / nodes
    grad_pos = -jax.nn.sigmoid(-s_pos) / nodes
    grad_neg = jax.nn.sigmoid(s_neg) / (NOISE * nodes)
    anchor = scale_factor * (
        grad_pos[:, None] * partner + jnp.dot(grad_neg, noise_emb, precision=highest)
    )
    partner_grad = jnp.dot(pairing.T, scale_factor * grad_pos[:, None] * zeta, precision=highest)
    dnoise = scale_factor * jnp.dot(grad_neg.T, zeta, precision=highest)
    groups = lax.axis_size("row")
    collected = lax.all_gather(dnoise.astype(jnp.bfloat16), "row", axis=0, tiled=True)
    owned = (noise_block_rows == my_row).astype(jnp.float32)
    returned = jnp.dot(
        owned[None, :],
        collected.astype(jnp.float32).reshape(groups, NOISE * width),
        precision=highest,
    )
    returned = returned.reshape(NOISE, width)
    dzeta = anchor + partner_grad
    dzeta = dzeta.at[:NOISE].add(returned)
    gpre = pull(dzeta)[0].astype(jnp.bfloat16)
    part_self = jnp.dot(node_feats.T, gpre, preferred_element_type=jnp.float32)
    neighbour_partial = jnp.dot(agg.T, gpre, preferred_element_type=jnp.float32)
    stacked = jnp.concatenate([part_self, neighbour_partial], axis=0)
    total, loss_tile = tree_allreduce(stacked, jnp.broadcast_to(loss_part, (8, 128)))
    grad_self = total[:width]
    neighbour_weight_gradient = total[width:]
    return (grad_self, neighbour_weight_gradient, loss_tile[0, 0])


def solution(mesh):
    in_specs = (
        P(("row", "col"), None),
        P("col", None),
        P(("row", "col"), None),
        P(("row", "col")),
        P(("row", "col"), None, None, None),
        P(("row", "col")),
        P(),
        P(),
        P(),
    )
    out_specs = (P(), P(), P())
    return jax.shard_map(body, mesh=mesh, in_specs=in_specs, out_specs=out_specs, check_vma=False)
```

profile of v0, /device:TPU:2, one launch (start us, length us, event | category | flops | bytes accessed | tf_op | source)
XLA Modules:
  0.0 480.4 jit_solution(14031274713754208656)
XLA Ops:
  10.2 66.5 %all-gather.4.cloned.1.call-done = bf16[4096,512]{1,0:T(8,128)(2,1)} async-done(((bf16[128,512]{1,0:T(8,128)(2,1)}), bf16[4096,512]{1,0:T(8,128)(2,1)}) %all-gather.4.cloned.1.call-update) | async-done | bytes 4194320 | tf_op jit(solution)/shard_map/all_gather | solution.py:76
  76.7 5.5 %fusion.1 = bf16[4,8,128,512]{3,1,2,0:T(8,128)(2,1)S(1)} fusion(bf16[32,128,512,1]{2,1,0,3:T(8,128)(2,1)} %bitcast.40, s32[4,8]{1,0:T(4,128)S(1)} %copy-done.5), kind=kOutput, calls=%fused_computation.2 | convolution fusion | flops 134218752 | bytes 8388736 | tf_op jit(solution)/shard_map/bkc,cjd->bkjd/dot_general | solution.py:82
  82.3 2.6 fusion.8
  87.9 77.2 %all-gather.6.cloned.1.call-done = bf16[2048,512]{0,1:T(8,128)(2,1)} async-done(((bf16[128,512]{0,1:T(8,128)(2,1)}), bf16[2048,512]{0,1:T(8,128)(2,1)}) %all-gather.6.cloned.1.call-update) | async-done | bytes 2097168 | tf_op jit(solution)/shard_map/all_gather | solution.py:92
  172.4 65.5 %all-gather.8.cloned.1.call-done = bf16[2048,512]{1,0:T(8,128)(2,1)} async-done(((bf16[128,512]{1,0:T(8,128)(2,1)}), bf16[2048,512]{1,0:T(8,128)(2,1)}) %all-gather.8.cloned.1.call-update) | async-done | bytes 2097168 | tf_op jit(solution)/shard_map/all_gather | solution.py:110
  238.0 3.1 reshape.99
  248.8 2.9 collective-permute-done
  254.4 2.5 collective-permute-start.1
  256.9 13.3 %collective-permute-done.1 = f32[256,512]{1,0:T(8,128)S(1)} collective-permute-done((f32[256,512]{1,0:T(8,128)S(1)}, f32[256,512]{1,0:T(8,128)S(1)}, u32[]{:S(2)}, u32[]{:S(2)}) %collective-permute-start.1) | collective-permute-done | bytes 524320 | tf_op jit(solution)/shard_map/ppermute | solution.py:38
  271.4 4.0 collective-permute-start.2
  275.4 6.9 %collective-permute-done.2 = f32[128,512]{1,0:T(8,128)S(1)} collective-permute-done((f32[128,512]{1,0:T(8,128)S(1)}, f32[128,512]{1,0:T(8,128)S(1)}, u32[]{:S(2)}, u32[]{:S(2)}) %collective-permute-start.2) | collective-permute-done | bytes 262176 | tf_op jit(solution)/shard_map/ppermute | solution.py:38
  282.4 3.4 collective-permute-start.3
  285.8 3.4 collective-permute-done.3
  289.3 4.9 %collective-permute-start.4 = (f32[32,512]{1,0:T(8,128)S(1)}, f32[32,512]{1,0:T(8,128)S(1)}, u32[]{:S(2)}, u32[]{:S(2)}) collective-permute-start(f32[32,512]{1,0:T(8,128)S(1)} %constant_dynamic-slice_fusion.6), channel_id=1, source_target_pairs={{0,16},{1,17},{2,18},{3,19},{4,20},{5,21},{6,22},{7,23},{8,24},{9,... | collective-permute-start | bytes 196616 | tf_op jit(solution)/shard_map/ppermute | solution.py:38
  294.2 2.7 collective-permute-done.4
  297.0 3.6 collective-permute-start.5
  302.8 3.4 collective-permute-start.6
  306.2 3.1 collective-permute-done.6
  309.3 5.1 %collective-permute-start.7 = (f32[4,512]{1,0:T(4,128)S(1)}, f32[4,512]{1,0:T(4,128)S(1)}, u32[]{:S(2)}, u32[]{:S(2)}) collective-permute-start(f32[4,512]{1,0:T(4,128)S(1)} %constant_dynamic-slice_fusion.2), channel_id=1, source_target_pairs={{0,128},{32,160},{64,192},{96,224},{128,0},{160,32},{192,64},{224,... | collective-permute-start | bytes 24584 | tf_op jit(solution)/shard_map/ppermute | solution.py:38
  314.5 4.3 collective-permute-done.7
  318.8 8.6 %collective-permute-start.8 = (f32[2,512]{1,0:T(2,128)S(1)}, f32[2,512]{1,0:T(2,128)S(1)}, u32[]{:S(2)}, u32[]{:S(2)}) collective-permute-start(f32[2,512]{1,0:T(2,128)S(1)} %constant_dynamic-slice_fusion), channel_id=1, source_target_pairs={{0,256},{32,288},{64,320},{96,352},{128,384},{160,416},{192,448},{... | collective-permute-start | bytes 12296 | tf_op jit(solution)/shard_map/ppermute | solution.py:38
  327.4 5.6 %collective-permute-done.8 = f32[2,512]{1,0:T(2,128)S(1)} collective-permute-done((f32[2,512]{1,0:T(2,128)S(1)}, f32[2,512]{1,0:T(2,128)S(1)}, u32[]{:S(2)}, u32[]{:S(2)}) %collective-permute-start.8) | collective-permute-done | bytes 4128 | tf_op jit(solution)/shard_map/ppermute | solution.py:38
  333.0 8.6 %collective-permute-start.9 = (f32[2,512]{1,0:T(2,128)S(1)}, f32[2,512]{1,0:T(2,128)S(1)}, u32[]{:S(2)}, u32[]{:S(2)}) collective-permute-start(f32[2,512]{1,0:T(2,128)S(1)} %get-tuple-element.16), channel_id=1, source_target_pairs={{0,256},{32,288},{64,320},{96,352},{128,384},{160,416},{192,448},{... | collective-permute-start | bytes 12296 | tf_op jit(solution)/shard_map/ppermute | solution.py:44
  341.7 5.6 %collective-permute-done.9 = f32[2,512]{1,0:T(2,128)S(1)} collective-permute-done((f32[2,512]{1,0:T(2,128)S(1)}, f32[2,512]{1,0:T(2,128)S(1)}, u32[]{:S(2)}, u32[]{:S(2)}) %collective-permute-start.9) | collective-permute-done | bytes 4128 | tf_op jit(solution)/shard_map/ppermute | solution.py:44
  347.3 5.1 %collective-permute-start.10 = (f32[4,512]{1,0:T(4,128)S(1)}, f32[4,512]{1,0:T(4,128)S(1)}, u32[]{:S(2)}, u32[]{:S(2)}) collective-permute-start(f32[4,512]{1,0:T(4,128)S(1)} %constant_dynamic-update-slice_fusion.16), channel_id=1, source_target_pairs={{0,128},{32,160},{64,192},{96,224},{128,0},{160,32},{192,64},{224,... | collective-permute-start | bytes 24584 | tf_op jit(solution)/shard_map/ppermute | solution.py:44
  352.4 4.3 collective-permute-done.10
  356.7 3.4 collective-permute-start.11
  360.1 3.1 collective-permute-done.11
  363.2 3.6 collective-permute-start.12
  369.0 4.9 %collective-permute-start.13 = (f32[32,512]{1,0:T(8,128)S(1)}, f32[32,512]{1,0:T(8,128)S(1)}, u32[]{:S(2)}, u32[]{:S(2)}) collective-permute-start(f32[32,512]{1,0:T(8,128)S(1)} %constant_dynamic-update-slice_fusion.10), channel_id=1, source_target_pairs={{0,16},{1,17},{2,18},{3,19},{4,20},{5,21},{6,22},{7,23},{8,24},{9,... | collective-permute-start | bytes 196616 | tf_op jit(solution)/shard_map/ppermute | solution.py:44
  374.0 2.7 collective-permute-done.13
  376.7 3.4 collective-permute-start.14
  380.1 3.4 collective-permute-done.14
  383.6 4.0 collective-permute-start.15
  387.6 5.7 %collective-permute-done.15 = f32[128,512]{1,0:T(8,128)S(1)} collective-permute-done((f32[128,512]{1,0:T(8,128)S(1)}, f32[128,512]{1,0:T(8,128)S(1)}, u32[]{:S(2)}, u32[]{:S(2)}) %collective-permute-start.15) | collective-permute-done | bytes 262176 | tf_op jit(solution)/shard_map/ppermute | solution.py:44
  396.0 8.4 %collective-permute-done.16 = f32[256,512]{1,0:T(8,128)S(1)} collective-permute-done((f32[256,512]{1,0:T(8,128)S(1)}, f32[256,512]{1,0:T(8,128)S(1)}, u32[]{:S(2)}, u32[]{:S(2)}) %collective-permute-start.16) | collective-permute-done | bytes 524320 | tf_op jit(solution)/shard_map/ppermute | solution.py:44
  413.4 3.0 collective-permute-done.19
  416.4 4.0 collective-permute-start.20
  420.4 3.0 collective-permute-done.20
  423.4 3.4 collective-permute-start.21
  428.9 4.9 %collective-permute-start.22 = (f32[8,128]{1,0:T(8,128)S(1)}, f32[8,128]{1,0:T(8,128)S(1)}, u32[]{:S(2)}, u32[]{:S(2)}) collective-permute-start(f32[8,128]{1,0:T(8,128)S(1)} %add.274), channel_id=1, source_target_pairs={{0,16},{1,17},{2,18},{3,19},{4,20},{5,21},{6,22},{7,23},{8,24},{9,... | collective-permute-start | bytes 12296 | tf_op jit(solution)/shard_map/ppermute | solution.py:38
  435.9 3.6 collective-permute-start.23
  441.4 3.4 collective-permute-start.24
  444.8 3.0 collective-permute-done.24
  447.8 5.1 %collective-permute-start.25 = (f32[8,128]{1,0:T(8,128)S(1)}, f32[8,128]{1,0:T(8,128)S(1)}, u32[]{:S(2)}, u32[]{:S(2)}) collective-permute-start(f32[8,128]{1,0:T(8,128)S(1)} %add.277), channel_id=1, source_target_pairs={{0,128},{32,160},{64,192},{96,224},{128,0},{160,32},{192,64},{224,... | collective-permute-start | bytes 12296 | tf_op jit(solution)/shard_map/ppermute | solution.py:38
  452.9 4.3 collective-permute-done.25
  457.2 8.7 %collective-permute-start.26 = (f32[8,128]{1,0:T(8,128)S(1)}, f32[8,128]{1,0:T(8,128)S(1)}, u32[]{:S(2)}, u32[]{:S(2)}) collective-permute-start(f32[8,128]{1,0:T(8,128)S(1)} %add.278), channel_id=1, source_target_pairs={{0,256},{32,288},{64,320},{96,352},{128,384},{160,416},{192,448},{... | collective-permute-start | bytes 12296 | tf_op jit(solution)/shard_map/ppermute | solution.py:38
  465.9 5.5 %collective-permute-done.26 = f32[8,128]{1,0:T(8,128)S(1)} collective-permute-done((f32[8,128]{1,0:T(8,128)S(1)}, f32[8,128]{1,0:T(8,128)S(1)}, u32[]{:S(2)}, u32[]{:S(2)}) %collective-permute-start.26) | collective-permute-done | bytes 4128 | tf_op jit(solution)/shard_map/ppermute | solution.py:38
  (113 shorter events, 47.5 us)
Async XLA Ops:
  7.2 1.5 copy-start
  7.2 69.5 %copy-start.5 = (s32[4,8]{1,0:T(4,128)S(1)}, s32[4,8]{1,0:T(4,128)}, u32[]{:S(2)}) copy-start(s32[4,8]{1,0:T(4,128)} %param.13) | copy-start | bytes 388
  7.2 69.5 %all-gather.4.cloned.1.call-start = ((), (), s32[]{:S(2)}) async-start(), calls=%async_computation | async-start | bytes 4325376 | tf_op jit(solution)/shard_map/all_gather | solution.py:76
  7.9 157.1 %all-gather.6.cloned.1.call-start = ((), (), s32[]{:S(2)}) async-start(), calls=%async_computation.1 | async-start | bytes 2228224 | tf_op jit(solution)/shard_map/all_gather | solution.py:92
  76.7 5.5 %copy-start.8 = (bf16[4,8,128,128]{3,2,1,0:T(8,128)(2,1)S(1)}, bf16[4,8,128,128]{3,2,1,0:T(8,128)(2,1)}, u32[]{:S(2)}) copy-start(bf16[4,8,128,128]{3,2,1,0:T(8,128)(2,1)} %param.15) | copy-start | bytes 3145732
  82.3 2.6 copy-start.4
  84.9 0.8 copy-start.2
  84.9 1.7 copy-start.7
  85.7 82.7 %copy-start.6 = (s32[512]{0:T(512)S(1)}, s32[512]{0:T(512)}, u32[]{:S(2)}) copy-start(s32[512]{0:T(512)} %param.16) | copy-start | bytes 6148
  86.4 151.6 %all-gather.8.cloned.1.call-start = ((), (), s32[]{:S(2)}) async-start(), calls=%async_computation.2 | async-start | bytes 2228224 | tf_op jit(solution)/shard_map/all_gather | solution.py:110
  243.4 1.0 copy-start.3
  246.8 4.9 %collective-permute-start = (f32[512,512]{1,0:T(8,128)}, f32[512,512]{1,0:T(8,128)}, u32[]{:S(2)}, u32[]{:S(2)}) collective-permute-start(f32[512,512]{1,0:T(8,128)} %fusion.12), channel_id=1, source_target_pairs={{0,1},{1,0},{2,3},{3,2},{4,5},{5,4},{6,7},{7,6},{8,9},{9,8},{10,11... | collective-permute-start | bytes 3145736 | tf_op jit(solution)/shard_map/ppermute | solution.py:38
  253.3 1.0 copy-start.1
  254.4 15.9 %collective-permute-start.1 = (f32[256,512]{1,0:T(8,128)S(1)}, f32[256,512]{1,0:T(8,128)S(1)}, u32[]{:S(2)}, u32[]{:S(2)}) collective-permute-start(f32[256,512]{1,0:T(8,128)S(1)} %constant_dynamic-slice_fusion.9), channel_id=1, source_target_pairs={{0,2},{1,3},{2,0},{3,1},{4,6},{5,7},{6,4},{7,5},{8,10},{9,11},{10,... | collective-permute-start | bytes 1572872 | tf_op jit(solution)/shard_map/ppermute | solution.py:38
  271.4 10.9 %collective-permute-start.2 = (f32[128,512]{1,0:T(8,128)S(1)}, f32[128,512]{1,0:T(8,128)S(1)}, u32[]{:S(2)}, u32[]{:S(2)}) collective-permute-start(f32[128,512]{1,0:T(8,128)S(1)} %constant_dynamic-slice_fusion.8), channel_id=1, source_target_pairs={{0,4},{1,5},{2,6},{3,7},{4,0},{5,1},{6,2},{7,3},{8,12},{9,13},{10,... | collective-permute-start | bytes 786440 | tf_op jit(solution)/shard_map/ppermute | solution.py:38
  282.4 6.9 %collective-permute-start.3 = (f32[64,512]{1,0:T(8,128)S(1)}, f32[64,512]{1,0:T(8,128)S(1)}, u32[]{:S(2)}, u32[]{:S(2)}) collective-permute-start(f32[64,512]{1,0:T(8,128)S(1)} %constant_dynamic-slice_fusion.7), channel_id=1, source_target_pairs={{0,8},{1,9},{2,10},{3,11},{4,12},{5,13},{6,14},{7,15},{8,0},{9,1},... | collective-permute-start | bytes 393224 | tf_op jit(solution)/shard_map/ppermute | solution.py:38
  289.3 7.7 %collective-permute-start.4 = (f32[32,512]{1,0:T(8,128)S(1)}, f32[32,512]{1,0:T(8,128)S(1)}, u32[]{:S(2)}, u32[]{:S(2)}) collective-permute-start(f32[32,512]{1,0:T(8,128)S(1)} %constant_dynamic-slice_fusion.6), channel_id=1, source_target_pairs={{0,16},{1,17},{2,18},{3,19},{4,20},{5,21},{6,22},{7,23},{8,24},{9,... | collective-permute-start | bytes 196616 | tf_op jit(solution)/shard_map/ppermute | solution.py:38
  297.0 5.8 %collective-permute-start.5 = (f32[16,512]{1,0:T(8,128)S(1)}, f32[16,512]{1,0:T(8,128)S(1)}, u32[]{:S(2)}, u32[]{:S(2)}) collective-permute-start(f32[16,512]{1,0:T(8,128)S(1)} %constant_dynamic-slice_fusion.5), channel_id=1, source_target_pairs={{0,32},{32,0},{64,96},{96,64},{128,160},{160,128},{192,224},{224,1... | collective-permute-start | bytes 98312 | tf_op jit(solution)/shard_map/ppermute | solution.py:38
  302.8 6.5 %collective-permute-start.6 = (f32[8,512]{1,0:T(8,128)S(1)}, f32[8,512]{1,0:T(8,128)S(1)}, u32[]{:S(2)}, u32[]{:S(2)}) collective-permute-start(f32[8,512]{1,0:T(8,128)S(1)} %constant_dynamic-slice_fusion.4), channel_id=1, source_target_pairs={{0,64},{32,96},{64,0},{96,32},{128,192},{160,224},{192,128},{224,1... | collective-permute-start | bytes 49160 | tf_op jit(solution)/shard_map/ppermute | solution.py:38
  309.3 9.5 %collective-permute-start.7 = (f32[4,512]{1,0:T(4,128)S(1)}, f32[4,512]{1,0:T(4,128)S(1)}, u32[]{:S(2)}, u32[]{:S(2)}) collective-permute-start(f32[4,512]{1,0:T(4,128)S(1)} %constant_dynamic-slice_fusion.2), channel_id=1, source_target_pairs={{0,128},{32,160},{64,192},{96,224},{128,0},{160,32},{192,64},{224,... | collective-permute-start | bytes 24584 | tf_op jit(solution)/shard_map/ppermute | solution.py:38
  318.8 14.2 %collective-permute-start.8 = (f32[2,512]{1,0:T(2,128)S(1)}, f32[2,512]{1,0:T(2,128)S(1)}, u32[]{:S(2)}, u32[]{:S(2)}) collective-permute-start(f32[2,512]{1,0:T(2,128)S(1)} %constant_dynamic-slice_fusion), channel_id=1, source_target_pairs={{0,256},{32,288},{64,320},{96,352},{128,384},{160,416},{192,448},{... | collective-permute-start | bytes 12296 | tf_op jit(solution)/shard_map/ppermute | solution.py:38
  333.0 14.2 %collective-permute-start.9 = (f32[2,512]{1,0:T(2,128)S(1)}, f32[2,512]{1,0:T(2,128)S(1)}, u32[]{:S(2)}, u32[]{:S(2)}) collective-permute-start(f32[2,512]{1,0:T(2,128)S(1)} %get-tuple-element.16), channel_id=1, source_target_pairs={{0,256},{32,288},{64,320},{96,352},{128,384},{160,416},{192,448},{... | collective-permute-start | bytes 12296 | tf_op jit(solution)/shard_map/ppermute | solution.py:44
  347.3 9.4 %collective-permute-start.10 = (f32[4,512]{1,0:T(4,128)S(1)}, f32[4,512]{1,0:T(4,128)S(1)}, u32[]{:S(2)}, u32[]{:S(2)}) collective-permute-start(f32[4,512]{1,0:T(4,128)S(1)} %constant_dynamic-update-slice_fusion.16), channel_id=1, source_target_pairs={{0,128},{32,160},{64,192},{96,224},{128,0},{160,32},{192,64},{224,... | collective-permute-start | bytes 24584 | tf_op jit(solution)/shard_map/ppermute | solution.py:44
  356.7 6.5 %collective-permute-start.11 = (f32[8,512]{1,0:T(8,128)S(1)}, f32[8,512]{1,0:T(8,128)S(1)}, u32[]{:S(2)}, u32[]{:S(2)}) collective-permute-start(f32[8,512]{1,0:T(8,128)S(1)} %constant_dynamic-update-slice_fusion.14), channel_id=1, source_target_pairs={{0,64},{32,96},{64,0},{96,32},{128,192},{160,224},{192,128},{224,1... | collective-permute-start | bytes 49160 | tf_op jit(solution)/shard_map/ppermute | solution.py:44
  363.2 5.8 %collective-permute-start.12 = (f32[16,512]{1,0:T(8,128)S(1)}, f32[16,512]{1,0:T(8,128)S(1)}, u32[]{:S(2)}, u32[]{:S(2)}) collective-permute-start(f32[16,512]{1,0:T(8,128)S(1)} %constant_dynamic-update-slice_fusion.12), channel_id=1, source_target_pairs={{0,32},{32,0},{64,96},{96,64},{128,160},{160,128},{192,224},{224,1... | collective-permute-start | bytes 98312 | tf_op jit(solution)/shard_map/ppermute | solution.py:44
  369.0 7.7 %collective-permute-start.13 = (f32[32,512]{1,0:T(8,128)S(1)}, f32[32,512]{1,0:T(8,128)S(1)}, u32[]{:S(2)}, u32[]{:S(2)}) collective-permute-start(f32[32,512]{1,0:T(8,128)S(1)} %constant_dynamic-update-slice_fusion.10), channel_id=1, source_target_pairs={{0,16},{1,17},{2,18},{3,19},{4,20},{5,21},{6,22},{7,23},{8,24},{9,... | collective-permute-start | bytes 196616 | tf_op jit(solution)/shard_map/ppermute | solution.py:44
  376.7 6.9 %collective-permute-start.14 = (f32[64,512]{1,0:T(8,128)S(1)}, f32[64,512]{1,0:T(8,128)S(1)}, u32[]{:S(2)}, u32[]{:S(2)}) collective-permute-start(f32[64,512]{1,0:T(8,128)S(1)} %constant_dynamic-update-slice_fusion.8), channel_id=1, source_target_pairs={{0,8},{1,9},{2,10},{3,11},{4,12},{5,13},{6,14},{7,15},{8,0},{9,1},... | collective-permute-start | bytes 393224 | tf_op jit(solution)/shard_map/ppermute | solution.py:44
  383.6 9.8 %collective-permute-start.15 = (f32[128,512]{1,0:T(8,128)S(1)}, f32[128,512]{1,0:T(8,128)S(1)}, u32[]{:S(2)}, u32[]{:S(2)}) collective-permute-start(f32[128,512]{1,0:T(8,128)S(1)} %constant_dynamic-update-slice_fusion.6), channel_id=1, source_target_pairs={{0,4},{1,5},{2,6},{3,7},{4,0},{5,1},{6,2},{7,3},{8,12},{9,13},{10,... | collective-permute-start | bytes 786440 | tf_op jit(solution)/shard_map/ppermute | solution.py:44
  393.4 11.1 %collective-permute-start.16 = (f32[256,512]{1,0:T(8,128)S(1)}, f32[256,512]{1,0:T(8,128)S(1)}, u32[]{:S(2)}, u32[]{:S(2)}) collective-permute-start(f32[256,512]{1,0:T(8,128)S(1)} %constant_dynamic-update-slice_fusion.4), channel_id=1, source_target_pairs={{0,2},{1,3},{2,0},{3,1},{4,6},{5,7},{6,4},{7,5},{8,10},{9,11},{10,... | collective-permute-start | bytes 1572872 | tf_op jit(solution)/shard_map/ppermute | solution.py:44
  404.5 67.8 %collective-permute-start.17 = (f32[512,512]{1,0:T(8,128)S(1)}, f32[512,512]{1,0:T(8,128)S(1)}, u32[]{:S(2)}, u32[]{:S(2)}) collective-permute-start(f32[512,512]{1,0:T(8,128)S(1)} %constant_dynamic-update-slice_fusion.2), channel_id=1, source_target_pairs={{0,1},{1,0},{2,3},{3,2},{4,5},{5,4},{6,7},{7,6},{8,9},{9,8},{10,11... | collective-permute-start | bytes 3145736 | tf_op jit(solution)/shard_map/ppermute | solution.py:44
  407.7 3.2 collective-permute-start.18
  410.9 5.5 %collective-permute-start.19 = (f32[8,128]{1,0:T(8,128)S(1)}, f32[8,128]{1,0:T(8,128)S(1)}, u32[]{:S(2)}, u32[]{:S(2)}) collective-permute-start(f32[8,128]{1,0:T(8,128)S(1)} %broadcast_add_fusion), channel_id=1, source_target_pairs={{0,2},{1,3},{2,0},{3,1},{4,6},{5,7},{6,4},{7,5},{8,10},{9,11},{10,... | collective-permute-start | bytes 12296 | tf_op jit(solution)/shard_map/ppermute | solution.py:38
  416.4 7.0 %collective-permute-start.20 = (f32[8,128]{1,0:T(8,128)S(1)}, f32[8,128]{1,0:T(8,128)S(1)}, u32[]{:S(2)}, u32[]{:S(2)}) collective-permute-start(f32[8,128]{1,0:T(8,128)S(1)} %fusion.56), channel_id=1, source_target_pairs={{0,4},{1,5},{2,6},{3,7},{4,0},{5,1},{6,2},{7,3},{8,12},{9,13},{10,... | collective-permute-start | bytes 12296 | tf_op jit(solution)/shard_map/ppermute | solution.py:38
  423.4 5.5 %collective-permute-start.21 = (f32[8,128]{1,0:T(8,128)S(1)}, f32[8,128]{1,0:T(8,128)S(1)}, u32[]{:S(2)}, u32[]{:S(2)}) collective-permute-start(f32[8,128]{1,0:T(8,128)S(1)} %add.273), channel_id=1, source_target_pairs={{0,8},{1,9},{2,10},{3,11},{4,12},{5,13},{6,14},{7,15},{8,0},{9,1},... | collective-permute-start | bytes 12296 | tf_op jit(solution)/shard_map/ppermute | solution.py:38
  428.9 7.0 %collective-permute-start.22 = (f32[8,128]{1,0:T(8,128)S(1)}, f32[8,128]{1,0:T(8,128)S(1)}, u32[]{:S(2)}, u32[]{:S(2)}) collective-permute-start(f32[8,128]{1,0:T(8,128)S(1)} %add.274), channel_id=1, source_target_pairs={{0,16},{1,17},{2,18},{3,19},{4,20},{5,21},{6,22},{7,23},{8,24},{9,... | collective-permute-start | bytes 12296 | tf_op jit(solution)/shard_map/ppermute | solution.py:38
  435.9 5.5 %collective-permute-start.23 = (f32[8,128]{1,0:T(8,128)S(1)}, f32[8,128]{1,0:T(8,128)S(1)}, u32[]{:S(2)}, u32[]{:S(2)}) collective-permute-start(f32[8,128]{1,0:T(8,128)S(1)} %add.275), channel_id=1, source_target_pairs={{0,32},{32,0},{64,96},{96,64},{128,160},{160,128},{192,224},{224,1... | collective-permute-start | bytes 12296 | tf_op jit(solution)/shard_map/ppermute | solution.py:38
  441.4 6.4 %collective-permute-start.24 = (f32[8,128]{1,0:T(8,128)S(1)}, f32[8,128]{1,0:T(8,128)S(1)}, u32[]{:S(2)}, u32[]{:S(2)}) collective-permute-start(f32[8,128]{1,0:T(8,128)S(1)} %add.276), channel_id=1, source_target_pairs={{0,64},{32,96},{64,0},{96,32},{128,192},{160,224},{192,128},{224,1... | collective-permute-start | bytes 12296 | tf_op jit(solution)/shard_map/ppermute | solution.py:38
  447.8 9.4 %collective-permute-start.25 = (f32[8,128]{1,0:T(8,128)S(1)}, f32[8,128]{1,0:T(8,128)S(1)}, u32[]{:S(2)}, u32[]{:S(2)}) collective-permute-start(f32[8,128]{1,0:T(8,128)S(1)} %add.277), channel_id=1, source_target_pairs={{0,128},{32,160},{64,192},{96,224},{128,0},{160,32},{192,64},{224,... | collective-permute-start | bytes 12296 | tf_op jit(solution)/shard_map/ppermute | solution.py:38
  457.2 14.2 %collective-permute-start.26 = (f32[8,128]{1,0:T(8,128)S(1)}, f32[8,128]{1,0:T(8,128)S(1)}, u32[]{:S(2)}, u32[]{:S(2)}) collective-permute-start(f32[8,128]{1,0:T(8,128)S(1)} %add.278), channel_id=1, source_target_pairs={{0,256},{32,288},{64,320},{96,352},{128,384},{160,416},{192,448},{... | collective-permute-start | bytes 12296 | tf_op jit(solution)/shard_map/ppermute | solution.py:38
Sparse Core Ops, SparseCore 0:
  11.2 65.5 all-gather.3
  86.5 78.5 all-gather.5
  168.5 69.4 all-gather.7
where the time goes:
time: 482 us; the launch traced here: 480 us
  waiting for transfers between devices  316 us (66%)
  starting transfers between devices  113 us (23%)
  matrix products  19.9 us (4%)
  between operations  16.7 us (3%)
  local copies, waits for them, and re-layouts  9.08 us (2%)
  other arithmetic  6.42 us (1%)
    all_gather x1, waiting for transfers between devices, body(): candidates = lax.all_gather(zeta_bf[:NOISE], 'row', axis=0, tiled=True)  77.2 us
    ppermute x18, starting transfers between devices, tree_allreduce(): got, got_extra = lax.ppermute((send, extra), axis, xor_pairs(size, mask))  75.2 us
    ppermute x18, waiting for transfers between devices, tree_allreduce(): got, got_extra = lax.ppermute((send, extra), axis, xor_pairs(size, mask))  70.2 us
    all_gather x1, waiting for transfers between devices, body(): piece = lax.all_gather(source_feats, 'col', axis=0, tiled=True)  66.5 us
    all_gather x1, waiting for transfers between devices, body(): lax.all_gather(dnoise.astype(jnp.bfloat16), 'row', axis=0, tiled=True)  65.5 us
    ppermute x9, starting transfers between devices, tree_allreduce(): got = lax.ppermute(buf, axis, xor_pairs(size, mask))  37.3 us
    ppermute x9, waiting for transfers between devices, tree_allreduce(): got = lax.ppermute(buf, axis, xor_pairs(size, mask))  35.4 us
  transfers between devices with their start and end apart: 30, of which 29 were waited for; matrix products, arithmetic and copies ran while one was open for 2% of the time, Pallas kernels for 0%

commit v1 on v0

--- a/solution.py
+++ b/solution.py
@@ -73,7 +73,9 @@
     scale_factor = 1.0 / softness_divisor
     valid = jnp.arange(slots, dtype=jnp.int32)[None, :] < nbr_count[:, None]
     tiles = adj_tiles * valid[:, :, None, None].astype(jnp.bfloat16)
-    piece = lax.all_gather(source_feats, "col", axis=0, tiled=True)
+    piece = jnp.concatenate(
+        lax.all_to_all(jnp.stack([source_feats] * lax.axis_size("col")), "col", 0, 0), axis=0
+    )
     count = piece.shape[0] // BLOCK
     blocks = piece.reshape(count, BLOCK, width)
     indicator_matrix = (

time: 482 us -> 477 us (0.990)
  waiting for transfers between devices: 316 us -> 298 us
  starting transfers between devices: 113 us -> 123 us
    all_gather x1 -> x0, waiting for transfers between devices: 66.5 us -> none  [body(): piece = lax.all_gather(source_feats, 'col', axis=0, tiled=True)]
    all_to_all x0 -> x1, waiting for transfers between devices: none -> 50.8 us  [body(): lax.all_to_all(jnp.stack([source_feats] * lax.axis_size('col')), 'col', 0...]
    all_to_all x0 -> x1, starting transfers between devices: none -> 10.5 us  [body(): lax.all_to_all(jnp.stack([source_feats] * lax.axis_size('col')), 'col', 0...]
  transfers between devices with their start and end apart: 30 -> 30, of which waited for: 29 -> 29; matrix products, arithmetic and copies ran while one was open for 2% -> 1% of each run, Pallas kernels for 0% -> 0%
where the time goes in v1:
time: 477 us; the launch traced here: 476 us
  waiting for transfers between devices  298 us (62%)
  starting transfers between devices  123 us (26%)
  matrix products  18.8 us (4%)
  between operations  17 us (4%)
  local copies, waits for them, and re-layouts  12.6 us (3%)
  other arithmetic  5.77 us (1%)
    all_gather x1, waiting for transfers between devices, body(): candidates = lax.all_gather(zeta_bf[:NOISE], 'row', axis=0, tiled=True)  76.4 us
    ppermute x18, starting transfers between devices, tree_allreduce(): got, got_extra = lax.ppermute((send, extra), axis, xor_pairs(size, mask))  75.2 us
    ppermute x18, waiting for transfers between devices, tree_allreduce(): got, got_extra = lax.ppermute((send, extra), axis, xor_pairs(size, mask))  70.2 us
    all_gather x1, waiting for transfers between devices, body(): lax.all_gather(dnoise.astype(jnp.bfloat16), 'row', axis=0, tiled=True)  65.6 us
    all_to_all x1, waiting for transfers between devices, body(): lax.all_to_all(jnp.stack([source_feats] * lax.axis_size('col')), 'col', 0...  50.8 us
    ppermute x9, starting transfers between devices, tree_allreduce(): got = lax.ppermute(buf, axis, xor_pairs(size, mask))  37.3 us
    ppermute x9, waiting for transfers between devices, tree_allreduce(): got = lax.ppermute(buf, axis, xor_pairs(size, mask))  35.4 us
    all_to_all x1, starting transfers between devices, body(): lax.all_to_all(jnp.stack([source_feats] * lax.axis_size('col')), 'col', 0...  10.5 us
  transfers between devices with their start and end apart: 30, of which 29 were waited for; matrix products, arithmetic and copies ran while one was open for 1% of the time, Pallas kernels for 0%

profile of v1, /device:TPU:2, one launch (start us, length us, event | category | flops | bytes accessed | tf_op | source)
XLA Modules:
  0.0 475.8 jit_solution(15777186208036326693)
XLA Ops:
  7.2 3.5 stack.2
  10.6 10.5 %all-to-all-start = ((bf16[32,128,512]{2,1,0:T(8,128)(2,1)}), bf16[32,128,512]{2,1,0:T(8,128)(2,1)}, u32[]{:S(2)}, u32[]{:S(2)}) async-start(bf16[32,128,512]{2,1,0:T(8,128)(2,1)} %stack.2), calls=%async_computation | async-start | bytes 8388608 | tf_op jit(solution)/shard_map/all_to_all | solution.py:77
  21.8 50.8 %all-to-all-done = bf16[32,128,512]{2,1,0:T(8,128)(2,1)} async-done(((bf16[32,128,512]{2,1,0:T(8,128)(2,1)}), bf16[32,128,512]{2,1,0:T(8,128)(2,1)}, u32[]{:S(2)}, u32[]{:S(2)}) %all-to-all-start) | async-done | bytes 4194336 | tf_op jit(solution)/shard_map/all_to_all | solution.py:77
  72.6 5.5 %fusion.1 = bf16[4,8,128,512]{3,1,2,0:T(8,128)(2,1)S(1)} fusion(bf16[32,128,512,1]{2,1,0,3:T(8,128)(2,1)} %bitcast.2, s32[4,8]{1,0:T(4,128)S(1)} %copy-done.6), kind=kOutput, calls=%fused_computation.2 | convolution fusion | flops 134218752 | bytes 8388736 | tf_op jit(solution)/shard_map/bkc,cjd->bkjd/dot_general | solution.py:84
  83.8 76.4 %all-gather.3.cloned.1.call-done = bf16[2048,512]{0,1:T(8,128)(2,1)} async-done(((bf16[128,512]{0,1:T(8,128)(2,1)}), bf16[2048,512]{0,1:T(8,128)(2,1)}) %all-gather.3.cloned.1.call-update) | async-done | bytes 2097168 | tf_op jit(solution)/shard_map/all_gather | solution.py:94
  167.5 65.6 %all-gather.5.cloned.1.call-done = bf16[2048,512]{1,0:T(8,128)(2,1)} async-done(((bf16[128,512]{1,0:T(8,128)(2,1)}), bf16[2048,512]{1,0:T(8,128)(2,1)}) %all-gather.5.cloned.1.call-update) | async-done | bytes 2097168 | tf_op jit(solution)/shard_map/all_gather | solution.py:112
  233.1 3.2 reshape.97
  243.9 2.9 collective-permute-done
  252.0 13.3 %collective-permute-done.1 = f32[256,512]{1,0:T(8,128)S(1)} collective-permute-done((f32[256,512]{1,0:T(8,128)S(1)}, f32[256,512]{1,0:T(8,128)S(1)}, u32[]{:S(2)}, u32[]{:S(2)}) %collective-permute-start.1) | collective-permute-done | bytes 524320 | tf_op jit(solution)/shard_map/ppermute | solution.py:38
  266.5 4.0 collective-permute-start.2
  270.5 6.9 %collective-permute-done.2 = f32[128,512]{1,0:T(8,128)S(1)} collective-permute-done((f32[128,512]{1,0:T(8,128)S(1)}, f32[128,512]{1,0:T(8,128)S(1)}, u32[]{:S(2)}, u32[]{:S(2)}) %collective-permute-start.2) | collective-permute-done | bytes 262176 | tf_op jit(solution)/shard_map/ppermute | solution.py:38
  277.5 3.4 collective-permute-start.3
  280.9 3.4 collective-permute-done.3
  284.4 4.9 %collective-permute-start.4 = (f32[32,512]{1,0:T(8,128)S(1)}, f32[32,512]{1,0:T(8,128)S(1)}, u32[]{:S(2)}, u32[]{:S(2)}) collective-permute-start(f32[32,512]{1,0:T(8,128)S(1)} %constant_dynamic-slice_fusion.6), channel_id=1, source_target_pairs={{0,16},{1,17},{2,18},{3,19},{4,20},{5,21},{6,22},{7,23},{8,24},{9,... | collective-permute-start | bytes 196616 | tf_op jit(solution)/shard_map/ppermute | solution.py:38
  289.3 2.7 collective-permute-done.4
  292.1 3.6 collective-permute-start.5
  297.9 3.4 collective-permute-start.6
  301.3 3.1 collective-permute-done.6
  304.4 5.1 %collective-permute-start.7 = (f32[4,512]{1,0:T(4,128)S(1)}, f32[4,512]{1,0:T(4,128)S(1)}, u32[]{:S(2)}, u32[]{:S(2)}) collective-permute-start(f32[4,512]{1,0:T(4,128)S(1)} %constant_dynamic-slice_fusion.2), channel_id=1, source_target_pairs={{0,128},{32,160},{64,192},{96,224},{128,0},{160,32},{192,64},{224,... | collective-permute-start | bytes 24584 | tf_op jit(solution)/shard_map/ppermute | solution.py:38
  309.6 4.3 collective-permute-done.7
  313.9 8.6 %collective-permute-start.8 = (f32[2,512]{1,0:T(2,128)S(1)}, f32[2,512]{1,0:T(2,128)S(1)}, u32[]{:S(2)}, u32[]{:S(2)}) collective-permute-start(f32[2,512]{1,0:T(2,128)S(1)} %constant_dynamic-slice_fusion), channel_id=1, source_target_pairs={{0,256},{32,288},{64,320},{96,352},{128,384},{160,416},{192,448},{... | collective-permute-start | bytes 12296 | tf_op jit(solution)/shard_map/ppermute | solution.py:38
  322.6 5.6 %collective-permute-done.8 = f32[2,512]{1,0:T(2,128)S(1)} collective-permute-done((f32[2,512]{1,0:T(2,128)S(1)}, f32[2,512]{1,0:T(2,128)S(1)}, u32[]{:S(2)}, u32[]{:S(2)}) %collective-permute-start.8) | collective-permute-done | bytes 4128 | tf_op jit(solution)/shard_map/ppermute | solution.py:38
  328.1 8.6 %collective-permute-start.9 = (f32[2,512]{1,0:T(2,128)S(1)}, f32[2,512]{1,0:T(2,128)S(1)}, u32[]{:S(2)}, u32[]{:S(2)}) collective-permute-start(f32[2,512]{1,0:T(2,128)S(1)} %get-tuple-element.16), channel_id=1, source_target_pairs={{0,256},{32,288},{64,320},{96,352},{128,384},{160,416},{192,448},{... | collective-permute-start | bytes 12296 | tf_op jit(solution)/shard_map/ppermute | solution.py:44
  336.8 5.6 %collective-permute-done.9 = f32[2,512]{1,0:T(2,128)S(1)} collective-permute-done((f32[2,512]{1,0:T(2,128)S(1)}, f32[2,512]{1,0:T(2,128)S(1)}, u32[]{:S(2)}, u32[]{:S(2)}) %collective-permute-start.9) | collective-permute-done | bytes 4128 | tf_op jit(solution)/shard_map/ppermute | solution.py:44
  342.4 5.1 %collective-permute-start.10 = (f32[4,512]{1,0:T(4,128)S(1)}, f32[4,512]{1,0:T(4,128)S(1)}, u32[]{:S(2)}, u32[]{:S(2)}) collective-permute-start(f32[4,512]{1,0:T(4,128)S(1)} %constant_dynamic-update-slice_fusion.16), channel_id=1, source_target_pairs={{0,128},{32,160},{64,192},{96,224},{128,0},{160,32},{192,64},{224,... | collective-permute-start | bytes 24584 | tf_op jit(solution)/shard_map/ppermute | solution.py:44
  347.5 4.3 collective-permute-done.10
  351.8 3.4 collective-permute-start.11
  355.2 3.1 collective-permute-done.11
  358.3 3.6 collective-permute-start.12
  364.1 4.9 %collective-permute-start.13 = (f32[32,512]{1,0:T(8,128)S(1)}, f32[32,512]{1,0:T(8,128)S(1)}, u32[]{:S(2)}, u32[]{:S(2)}) collective-permute-start(f32[32,512]{1,0:T(8,128)S(1)} %constant_dynamic-update-slice_fusion.10), channel_id=1, source_target_pairs={{0,16},{1,17},{2,18},{3,19},{4,20},{5,21},{6,22},{7,23},{8,24},{9,... | collective-permute-start | bytes 196616 | tf_op jit(solution)/shard_map/ppermute | solution.py:44
  369.1 2.7 collective-permute-done.13
  371.8 3.4 collective-permute-start.14
  375.3 3.4 collective-permute-done.14
  378.7 4.0 collective-permute-start.15
  382.8 5.7 %collective-permute-done.15 = f32[128,512]{1,0:T(8,128)S(1)} collective-permute-done((f32[128,512]{1,0:T(8,128)S(1)}, f32[128,512]{1,0:T(8,128)S(1)}, u32[]{:S(2)}, u32[]{:S(2)}) %collective-permute-start.15) | collective-permute-done | bytes 262176 | tf_op jit(solution)/shard_map/ppermute | solution.py:44
  391.1 8.4 %collective-permute-done.16 = f32[256,512]{1,0:T(8,128)S(1)} collective-permute-done((f32[256,512]{1,0:T(8,128)S(1)}, f32[256,512]{1,0:T(8,128)S(1)}, u32[]{:S(2)}, u32[]{:S(2)}) %collective-permute-start.16) | collective-permute-done | bytes 524320 | tf_op jit(solution)/shard_map/ppermute | solution.py:44
  408.5 3.0 collective-permute-done.19
  411.5 4.0 collective-permute-start.20
  415.5 3.0 collective-permute-done.20
  418.5 3.4 collective-permute-start.21
  424.0 4.9 %collective-permute-start.22 = (f32[8,128]{1,0:T(8,128)S(1)}, f32[8,128]{1,0:T(8,128)S(1)}, u32[]{:S(2)}, u32[]{:S(2)}) collective-permute-start(f32[8,128]{1,0:T(8,128)S(1)} %add.274), channel_id=1, source_target_pairs={{0,16},{1,17},{2,18},{3,19},{4,20},{5,21},{6,22},{7,23},{8,24},{9,... | collective-permute-start | bytes 12296 | tf_op jit(solution)/shard_map/ppermute | solution.py:38
  431.0 3.6 collective-permute-start.23
  436.5 3.4 collective-permute-start.24
  439.9 3.0 collective-permute-done.24
  442.9 5.1 %collective-permute-start.25 = (f32[8,128]{1,0:T(8,128)S(1)}, f32[8,128]{1,0:T(8,128)S(1)}, u32[]{:S(2)}, u32[]{:S(2)}) collective-permute-start(f32[8,128]{1,0:T(8,128)S(1)} %add.277), channel_id=1, source_target_pairs={{0,128},{32,160},{64,192},{96,224},{128,0},{160,32},{192,64},{224,... | collective-permute-start | bytes 12296 | tf_op jit(solution)/shard_map/ppermute | solution.py:38
  448.0 4.3 collective-permute-done.25
  452.3 8.7 %collective-permute-start.26 = (f32[8,128]{1,0:T(8,128)S(1)}, f32[8,128]{1,0:T(8,128)S(1)}, u32[]{:S(2)}, u32[]{:S(2)}) collective-permute-start(f32[8,128]{1,0:T(8,128)S(1)} %add.278), channel_id=1, source_target_pairs={{0,256},{32,288},{64,320},{96,352},{128,384},{160,416},{192,448},{... | collective-permute-start | bytes 12296 | tf_op jit(solution)/shard_map/ppermute | solution.py:38
  461.0 5.5 %collective-permute-done.26 = f32[8,128]{1,0:T(8,128)S(1)} collective-permute-done((f32[8,128]{1,0:T(8,128)S(1)}, f32[8,128]{1,0:T(8,128)S(1)}, u32[]{:S(2)}, u32[]{:S(2)}) %collective-permute-start.26) | collective-permute-done | bytes 4128 | tf_op jit(solution)/shard_map/ppermute | solution.py:38
  (117 shorter events, 50.1 us)
Async XLA Ops:
  7.2 14.1 %copy-start = (bf16[512,512]{1,0:T(8,128)(2,1)S(1)}, bf16[512,512]{1,0:T(8,128)(2,1)}, u32[]{:S(2)}) copy-start(bf16[512,512]{1,0:T(8,128)(2,1)} %param.11) | copy-start | bytes 1572868
  10.6 10.6 %copy-start.10 = (s32[4]{0:T(128)S(1)}, s32[4]{0:T(128)}, u32[]{:S(2)}) copy-start(s32[4]{0:T(128)} %param.14) | copy-start | bytes 52
  10.6 10.6 %copy-start.4 = (bf16[512,512]{1,0:T(8,128)(2,1)S(1)}, bf16[512,512]{1,0:T(8,128)(2,1)}, u32[]{:S(2)}) copy-start(bf16[512,512]{1,0:T(8,128)(2,1)} %param.18) | copy-start | bytes 1572868
  10.6 62.0 %all-to-all-start = ((bf16[32,128,512]{2,1,0:T(8,128)(2,1)}), bf16[32,128,512]{2,1,0:T(8,128)(2,1)}, u32[]{:S(2)}, u32[]{:S(2)}) async-start(bf16[32,128,512]{2,1,0:T(8,128)(2,1)} %stack.2), calls=%async_computation | async-start | bytes 8388608 | tf_op jit(solution)/shard_map/all_to_all | solution.py:77
  21.1 51.5 %copy-start.6 = (s32[4,8]{1,0:T(4,128)S(1)}, s32[4,8]{1,0:T(4,128)}, u32[]{:S(2)}) copy-start(s32[4,8]{1,0:T(4,128)} %param.13) | copy-start | bytes 388
  21.1 139.0 %all-gather.3.cloned.1.call-start = ((), (), s32[]{:S(2)}) async-start(), calls=%async_computation.1 | async-start | bytes 2228224 | tf_op jit(solution)/shard_map/all_gather | solution.py:94
  72.6 5.5 %copy-start.9 = (bf16[4,8,128,128]{3,2,1,0:T(8,128)(2,1)S(1)}, bf16[4,8,128,128]{3,2,1,0:T(8,128)(2,1)}, u32[]{:S(2)}) copy-start(bf16[4,8,128,128]{3,2,1,0:T(8,128)(2,1)} %param.15) | copy-start | bytes 3145732
  78.2 2.6 copy-start.5
  80.8 0.8 copy-start.2
  80.8 1.7 copy-start.8
  81.6 81.9 %copy-start.7 = (s32[512]{0:T(512)S(1)}, s32[512]{0:T(512)}, u32[]{:S(2)}) copy-start(s32[512]{0:T(512)} %param.16) | copy-start | bytes 6148
  82.3 150.8 %all-gather.5.cloned.1.call-start = ((), (), s32[]{:S(2)}) async-start(), calls=%async_computation.2 | async-start | bytes 2228224 | tf_op jit(solution)/shard_map/all_gather | solution.py:112
  238.5 1.0 copy-start.3
  241.9 4.9 %collective-permute-start = (f32[512,512]{1,0:T(8,128)}, f32[512,512]{1,0:T(8,128)}, u32[]{:S(2)}, u32[]{:S(2)}) collective-permute-start(f32[512,512]{1,0:T(8,128)} %fusion.12), channel_id=1, source_target_pairs={{0,1},{1,0},{2,3},{3,2},{4,5},{5,4},{6,7},{7,6},{8,9},{9,8},{10,11... | collective-permute-start | bytes 3145736 | tf_op jit(solution)/shard_map/ppermute | solution.py:38
  248.5 1.0 copy-start.1
  249.5 15.9 %collective-permute-start.1 = (f32[256,512]{1,0:T(8,128)S(1)}, f32[256,512]{1,0:T(8,128)S(1)}, u32[]{:S(2)}, u32[]{:S(2)}) collective-permute-start(f32[256,512]{1,0:T(8,128)S(1)} %constant_dynamic-slice_fusion.9), channel_id=1, source_target_pairs={{0,2},{1,3},{2,0},{3,1},{4,6},{5,7},{6,4},{7,5},{8,10},{9,11},{10,... | collective-permute-start | bytes 1572872 | tf_op jit(solution)/shard_map/ppermute | solution.py:38
  266.5 10.9 %collective-permute-start.2 = (f32[128,512]{1,0:T(8,128)S(1)}, f32[128,512]{1,0:T(8,128)S(1)}, u32[]{:S(2)}, u32[]{:S(2)}) collective-permute-start(f32[128,512]{1,0:T(8,128)S(1)} %constant_dynamic-slice_fusion.8), channel_id=1, source_target_pairs={{0,4},{1,5},{2,6},{3,7},{4,0},{5,1},{6,2},{7,3},{8,12},{9,13},{10,... | collective-permute-start | bytes 786440 | tf_op jit(solution)/shard_map/ppermute | solution.py:38
  277.5 6.9 %collective-permute-start.3 = (f32[64,512]{1,0:T(8,128)S(1)}, f32[64,512]{1,0:T(8,128)S(1)}, u32[]{:S(2)}, u32[]{:S(2)}) collective-permute-start(f32[64,512]{1,0:T(8,128)S(1)} %constant_dynamic-slice_fusion.7), channel_id=1, source_target_pairs={{0,8},{1,9},{2,10},{3,11},{4,12},{5,13},{6,14},{7,15},{8,0},{9,1},... | collective-permute-start | bytes 393224 | tf_op jit(solution)/shard_map/ppermute | solution.py:38
  284.4 7.7 %collective-permute-start.4 = (f32[32,512]{1,0:T(8,128)S(1)}, f32[32,512]{1,0:T(8,128)S(1)}, u32[]{:S(2)}, u32[]{:S(2)}) collective-permute-start(f32[32,512]{1,0:T(8,128)S(1)} %constant_dynamic-slice_fusion.6), channel_id=1, source_target_pairs={{0,16},{1,17},{2,18},{3,19},{4,20},{5,21},{6,22},{7,23},{8,24},{9,... | collective-permute-start | bytes 196616 | tf_op jit(solution)/shard_map/ppermute | solution.py:38
  292.1 5.8 %collective-permute-start.5 = (f32[16,512]{1,0:T(8,128)S(1)}, f32[16,512]{1,0:T(8,128)S(1)}, u32[]{:S(2)}, u32[]{:S(2)}) collective-permute-start(f32[16,512]{1,0:T(8,128)S(1)} %constant_dynamic-slice_fusion.5), channel_id=1, source_target_pairs={{0,32},{32,0},{64,96},{96,64},{128,160},{160,128},{192,224},{224,1... | collective-permute-start | bytes 98312 | tf_op jit(solution)/shard_map/ppermute | solution.py:38
  297.9 6.5 %collective-permute-start.6 = (f32[8,512]{1,0:T(8,128)S(1)}, f32[8,512]{1,0:T(8,128)S(1)}, u32[]{:S(2)}, u32[]{:S(2)}) collective-permute-start(f32[8,512]{1,0:T(8,128)S(1)} %constant_dynamic-slice_fusion.4), channel_id=1, source_target_pairs={{0,64},{32,96},{64,0},{96,32},{128,192},{160,224},{192,128},{224,1... | collective-permute-start | bytes 49160 | tf_op jit(solution)/shard_map/ppermute | solution.py:38
  304.4 9.5 %collective-permute-start.7 = (f32[4,512]{1,0:T(4,128)S(1)}, f32[4,512]{1,0:T(4,128)S(1)}, u32[]{:S(2)}, u32[]{:S(2)}) collective-permute-start(f32[4,512]{1,0:T(4,128)S(1)} %constant_dynamic-slice_fusion.2), channel_id=1, source_target_pairs={{0,128},{32,160},{64,192},{96,224},{128,0},{160,32},{192,64},{224,... | collective-permute-start | bytes 24584 | tf_op jit(solution)/shard_map/ppermute | solution.py:38
  313.9 14.2 %collective-permute-start.8 = (f32[2,512]{1,0:T(2,128)S(1)}, f32[2,512]{1,0:T(2,128)S(1)}, u32[]{:S(2)}, u32[]{:S(2)}) collective-permute-start(f32[2,512]{1,0:T(2,128)S(1)} %constant_dynamic-slice_fusion), channel_id=1, source_target_pairs={{0,256},{32,288},{64,320},{96,352},{128,384},{160,416},{192,448},{... | collective-permute-start | bytes 12296 | tf_op jit(solution)/shard_map/ppermute | solution.py:38
  328.1 14.2 %collective-permute-start.9 = (f32[2,512]{1,0:T(2,128)S(1)}, f32[2,512]{1,0:T(2,128)S(1)}, u32[]{:S(2)}, u32[]{:S(2)}) collective-permute-start(f32[2,512]{1,0:T(2,128)S(1)} %get-tuple-element.16), channel_id=1, source_target_pairs={{0,256},{32,288},{64,320},{96,352},{128,384},{160,416},{192,448},{... | collective-permute-start | bytes 12296 | tf_op jit(solution)/shard_map/ppermute | solution.py:44
  342.4 9.4 %collective-permute-start.10 = (f32[4,512]{1,0:T(4,128)S(1)}, f32[4,512]{1,0:T(4,128)S(1)}, u32[]{:S(2)}, u32[]{:S(2)}) collective-permute-start(f32[4,512]{1,0:T(4,128)S(1)} %constant_dynamic-update-slice_fusion.16), channel_id=1, source_target_pairs={{0,128},{32,160},{64,192},{96,224},{128,0},{160,32},{192,64},{224,... | collective-permute-start | bytes 24584 | tf_op jit(solution)/shard_map/ppermute | solution.py:44
  351.8 6.5 %collective-permute-start.11 = (f32[8,512]{1,0:T(8,128)S(1)}, f32[8,512]{1,0:T(8,128)S(1)}, u32[]{:S(2)}, u32[]{:S(2)}) collective-permute-start(f32[8,512]{1,0:T(8,128)S(1)} %constant_dynamic-update-slice_fusion.14), channel_id=1, source_target_pairs={{0,64},{32,96},{64,0},{96,32},{128,192},{160,224},{192,128},{224,1... | collective-permute-start | bytes 49160 | tf_op jit(solution)/shard_map/ppermute | solution.py:44
  358.3 5.8 %collective-permute-start.12 = (f32[16,512]{1,0:T(8,128)S(1)}, f32[16,512]{1,0:T(8,128)S(1)}, u32[]{:S(2)}, u32[]{:S(2)}) collective-permute-start(f32[16,512]{1,0:T(8,128)S(1)} %constant_dynamic-update-slice_fusion.12), channel_id=1, source_target_pairs={{0,32},{32,0},{64,96},{96,64},{128,160},{160,128},{192,224},{224,1... | collective-permute-start | bytes 98312 | tf_op jit(solution)/shard_map/ppermute | solution.py:44
  364.1 7.7 %collective-permute-start.13 = (f32[32,512]{1,0:T(8,128)S(1)}, f32[32,512]{1,0:T(8,128)S(1)}, u32[]{:S(2)}, u32[]{:S(2)}) collective-permute-start(f32[32,512]{1,0:T(8,128)S(1)} %constant_dynamic-update-slice_fusion.10), channel_id=1, source_target_pairs={{0,16},{1,17},{2,18},{3,19},{4,20},{5,21},{6,22},{7,23},{8,24},{9,... | collective-permute-start | bytes 196616 | tf_op jit(solution)/shard_map/ppermute | solution.py:44
  371.8 6.9 %collective-permute-start.14 = (f32[64,512]{1,0:T(8,128)S(1)}, f32[64,512]{1,0:T(8,128)S(1)}, u32[]{:S(2)}, u32[]{:S(2)}) collective-permute-start(f32[64,512]{1,0:T(8,128)S(1)} %constant_dynamic-update-slice_fusion.8), channel_id=1, source_target_pairs={{0,8},{1,9},{2,10},{3,11},{4,12},{5,13},{6,14},{7,15},{8,0},{9,1},... | collective-permute-start | bytes 393224 | tf_op jit(solution)/shard_map/ppermute | solution.py:44
  378.7 9.8 %collective-permute-start.15 = (f32[128,512]{1,0:T(8,128)S(1)}, f32[128,512]{1,0:T(8,128)S(1)}, u32[]{:S(2)}, u32[]{:S(2)}) collective-permute-start(f32[128,512]{1,0:T(8,128)S(1)} %constant_dynamic-update-slice_fusion.6), channel_id=1, source_target_pairs={{0,4},{1,5},{2,6},{3,7},{4,0},{5,1},{6,2},{7,3},{8,12},{9,13},{10,... | collective-permute-start | bytes 786440 | tf_op jit(solution)/shard_map/ppermute | solution.py:44
  388.5 11.1 %collective-permute-start.16 = (f32[256,512]{1,0:T(8,128)S(1)}, f32[256,512]{1,0:T(8,128)S(1)}, u32[]{:S(2)}, u32[]{:S(2)}) collective-permute-start(f32[256,512]{1,0:T(8,128)S(1)} %constant_dynamic-update-slice_fusion.4), channel_id=1, source_target_pairs={{0,2},{1,3},{2,0},{3,1},{4,6},{5,7},{6,4},{7,5},{8,10},{9,11},{10,... | collective-permute-start | bytes 1572872 | tf_op jit(solution)/shard_map/ppermute | solution.py:44
  399.6 67.8 %collective-permute-start.17 = (f32[512,512]{1,0:T(8,128)S(1)}, f32[512,512]{1,0:T(8,128)S(1)}, u32[]{:S(2)}, u32[]{:S(2)}) collective-permute-start(f32[512,512]{1,0:T(8,128)S(1)} %constant_dynamic-update-slice_fusion.2), channel_id=1, source_target_pairs={{0,1},{1,0},{2,3},{3,2},{4,5},{5,4},{6,7},{7,6},{8,9},{9,8},{10,11... | collective-permute-start | bytes 3145736 | tf_op jit(solution)/shard_map/ppermute | solution.py:44
  402.8 3.2 collective-permute-start.18
  406.1 5.5 %collective-permute-start.19 = (f32[8,128]{1,0:T(8,128)S(1)}, f32[8,128]{1,0:T(8,128)S(1)}, u32[]{:S(2)}, u32[]{:S(2)}) collective-permute-start(f32[8,128]{1,0:T(8,128)S(1)} %broadcast_add_fusion), channel_id=1, source_target_pairs={{0,2},{1,3},{2,0},{3,1},{4,6},{5,7},{6,4},{7,5},{8,10},{9,11},{10,... | collective-permute-start | bytes 12296 | tf_op jit(solution)/shard_map/ppermute | solution.py:38
  411.5 7.0 %collective-permute-start.20 = (f32[8,128]{1,0:T(8,128)S(1)}, f32[8,128]{1,0:T(8,128)S(1)}, u32[]{:S(2)}, u32[]{:S(2)}) collective-permute-start(f32[8,128]{1,0:T(8,128)S(1)} %fusion.56), channel_id=1, source_target_pairs={{0,4},{1,5},{2,6},{3,7},{4,0},{5,1},{6,2},{7,3},{8,12},{9,13},{10,... | collective-permute-start | bytes 12296 | tf_op jit(solution)/shard_map/ppermute | solution.py:38
  418.5 5.5 %collective-permute-start.21 = (f32[8,128]{1,0:T(8,128)S(1)}, f32[8,128]{1,0:T(8,128)S(1)}, u32[]{:S(2)}, u32[]{:S(2)}) collective-permute-start(f32[8,128]{1,0:T(8,128)S(1)} %add.273), channel_id=1, source_target_pairs={{0,8},{1,9},{2,10},{3,11},{4,12},{5,13},{6,14},{7,15},{8,0},{9,1},... | collective-permute-start | bytes 12296 | tf_op jit(solution)/shard_map/ppermute | solution.py:38
  424.0 7.0 %collective-permute-start.22 = (f32[8,128]{1,0:T(8,128)S(1)}, f32[8,128]{1,0:T(8,128)S(1)}, u32[]{:S(2)}, u32[]{:S(2)}) collective-permute-start(f32[8,128]{1,0:T(8,128)S(1)} %add.274), channel_id=1, source_target_pairs={{0,16},{1,17},{2,18},{3,19},{4,20},{5,21},{6,22},{7,23},{8,24},{9,... | collective-permute-start | bytes 12296 | tf_op jit(solution)/shard_map/ppermute | solution.py:38
  431.0 5.5 %collective-permute-start.23 = (f32[8,128]{1,0:T(8,128)S(1)}, f32[8,128]{1,0:T(8,128)S(1)}, u32[]{:S(2)}, u32[]{:S(2)}) collective-permute-start(f32[8,128]{1,0:T(8,128)S(1)} %add.275), channel_id=1, source_target_pairs={{0,32},{32,0},{64,96},{96,64},{128,160},{160,128},{192,224},{224,1... | collective-permute-start | bytes 12296 | tf_op jit(solution)/shard_map/ppermute | solution.py:38
  436.5 6.4 %collective-permute-start.24 = (f32[8,128]{1,0:T(8,128)S(1)}, f32[8,128]{1,0:T(8,128)S(1)}, u32[]{:S(2)}, u32[]{:S(2)}) collective-permute-start(f32[8,128]{1,0:T(8,128)S(1)} %add.276), channel_id=1, source_target_pairs={{0,64},{32,96},{64,0},{96,32},{128,192},{160,224},{192,128},{224,1... | collective-permute-start | bytes 12296 | tf_op jit(solution)/shard_map/ppermute | solution.py:38
  442.9 9.4 %collective-permute-start.25 = (f32[8,128]{1,0:T(8,128)S(1)}, f32[8,128]{1,0:T(8,128)S(1)}, u32[]{:S(2)}, u32[]{:S(2)}) collective-permute-start(f32[8,128]{1,0:T(8,128)S(1)} %add.277), channel_id=1, source_target_pairs={{0,128},{32,160},{64,192},{96,224},{128,0},{160,32},{192,64},{224,... | collective-permute-start | bytes 12296 | tf_op jit(solution)/shard_map/ppermute | solution.py:38
  452.3 14.2 %collective-permute-start.26 = (f32[8,128]{1,0:T(8,128)S(1)}, f32[8,128]{1,0:T(8,128)S(1)}, u32[]{:S(2)}, u32[]{:S(2)}) collective-permute-start(f32[8,128]{1,0:T(8,128)S(1)} %add.278), channel_id=1, source_target_pairs={{0,256},{32,288},{64,320},{96,352},{128,384},{160,416},{192,448},{... | collective-permute-start | bytes 12296 | tf_op jit(solution)/shard_map/ppermute | solution.py:38
Sparse Core Ops, SparseCore 0:
  82.4 77.7 all-gather.2
  163.6 69.4 all-gather.4
